TPU v7x, 256 devices: a whole 4x4x8 slice. The times are simulated.
256 devices in a mesh: rep: 8 (over z), shard: 32 (over y, x, core).
Axes of the slice: x: 4, y: 4, z: 8, core: 2. Of those that a mesh axis runs over, the one named last changes fastest.
Arguments:
- grad_joined: bfloat16 [8, 1024, 3072], P('rep', 'shard')
- error_joined: float32 [8, 1024, 3072], P('rep', 'shard'), may hold values from -6 to 6
- moment_joined: float32 [1024, 3072], P('shard'), may hold values from -6 to 6
- weight_joined: float32 [1024, 3072], P('shard'), may hold values from -0.1875 to 0.1875
- factor_joined: float32 [32, 3072], replicated, may hold values from -6 to 6
- grad_dense: bfloat16 [8, 1024, 1024], P('rep', 'shard')
- error_dense: float32 [8, 1024, 1024], P('rep', 'shard'), may hold values from -6 to 6
- moment_dense: float32 [1024, 1024], P('shard'), may hold values from -6 to 6
- weight_dense: float32 [1024, 1024], P('shard'), may hold values from -0.1875 to 0.1875
- factor_dense: float32 [32, 1024], replicated, may hold values from -6 to 6
- grad_expand: bfloat16 [8, 1024, 4096], P('rep', 'shard')
- error_expand: float32 [8, 1024, 4096], P('rep', 'shard'), may hold values from -6 to 6
- moment_expand: float32 [1024, 4096], P('shard'), may hold values from -6 to 6
- weight_expand: float32 [1024, 4096], P('shard'), may hold values from -0.1875 to 0.1875
- factor_expand: float32 [32, 4096], replicated, may hold values from -6 to 6
- grad_shrink: bfloat16 [8, 4096, 1024], P('rep', 'shard')
- error_shrink: float32 [8, 4096, 1024], P('rep', 'shard'), may hold values from -6 to 6
- moment_shrink: float32 [4096, 1024], P('shard'), may hold values from -6 to 6
- weight_shrink: float32 [4096, 1024], P('shard'), may hold values from -0.09375 to 0.09375
- factor_shrink: float32 [32, 1024], replicated, may hold values from -6 to 6
- vector_grad: bfloat16 [8, 13312], P('rep', 'shard'), may hold values from -6 to 6
- vector_moment: float32 [13312], P('shard'), may hold values from -6 to 6
- vector_weight: float32 [13312], P('shard'), may hold values from -1.5 to 1.5
Outputs:
- errors_joined: float32 [8, 1024, 3072], P('rep', 'shard')
- moments_joined: float32 [1024, 3072], P('shard')
- weights_joined: float32 [1024, 3072], P('shard')
- factors_joined: float32 [32, 3072], replicated
- errors_dense: float32 [8, 1024, 1024], P('rep', 'shard')
- moments_dense: float32 [1024, 1024], P('shard')
- weights_dense: float32 [1024, 1024], P('shard')
- factors_dense: float32 [32, 1024], replicated
- errors_expand: float32 [8, 1024, 4096], P('rep', 'shard')
- moments_expand: float32 [1024, 4096], P('shard')
- weights_expand: float32 [1024, 4096], P('shard')
- factors_expand: float32 [32, 4096], replicated
- errors_shrink: float32 [8, 4096, 1024], P('rep', 'shard')
- moments_shrink: float32 [4096, 1024], P('shard')
- weights_shrink: float32 [4096, 1024], P('shard')
- factors_shrink: float32 [32, 1024], replicated
- vector_moments: float32 [13312], P('shard')
- vector_weights: float32 [13312], P('shard')
All inputs are finite; a program needn't handle non-finite values.
Results may differ from a plain program's by a relative error of at most 0.0003.
Values sent between devices are 32-bit elements; how exact they have to be, the bound alone decides.
No kernel may reach another device: no remote copies, remote signals or barrier semaphores. Data moves between devices by JAX's collectives and lax.ppermute only.
A program may use at most 128 MiB of HBM per device.

v0:
```python
import jax
import jax.numpy as jnp
from jax import lax
from jax.sharding import PartitionSpec as P

ROUNDS = 2


HIGHEST_PRECISION = lax.Precision.HIGHEST
momentum_decay = 0.9
learn_rate = 0.1


def row_product(factor, matrix):
    return lax.dot_general(
        factor,
        matrix,
        (((1,), (1,)), ((), ())),
        precision=HIGHEST_PRECISION,
        preferred_element_type=jnp.float32,
    )


def gram_of(row_factor):
    return lax.dot_general(
        row_factor,
        row_factor,
        (((1,), (1,)), ((), ())),
        precision=HIGHEST_PRECISION,
        preferred_element_type=jnp.float32,
    )


def mat(a, b):
    return jnp.dot(a, b, precision=HIGHEST_PRECISION, preferred_element_type=jnp.float32)


def inverse_cholesky(grams):
    lower = jnp.linalg.cholesky(grams)
    eye = jnp.broadcast_to(jnp.eye(grams.shape[-1], dtype=grams.dtype), grams.shape)
    return lax.linalg.triangular_solve(lower, eye, left_side=True, lower=True)


def exchange(x, axis, size, bit):
    return lax.ppermute(x, axis, [(s, s ^ (1 << bit)) for s in range(size)])


def doubling_sum(values, axis):
    size = lax.axis_size(axis)
    flat = jnp.concatenate([v.reshape(-1) for v in values])
    count = flat.shape[0]
    padded = -(-count // 1024) * 1024
    block = jnp.pad(flat, (0, padded - count)).reshape(-1, 128)
    for bit in range(size.bit_length() - 1):
        block = block + exchange(block, axis, size, bit)
    flat = block.reshape(-1)
    out, start = [], 0
    for v in values:
        out.append(flat[start : start + v.size].reshape(v.shape))
        start += v.size
    return tuple(out)


def halving_steps(sizes):
    shard_bits = sizes["shard"].bit_length() - 1
    rep_bits = sizes["rep"].bit_length() - 1
    preferred = [("shard", 0), ("shard", 1), ("shard", 3), ("rep", 0),
                 ("shard", 2), ("shard", 4), ("rep", 1), ("rep", 2)]
    steps = [(a, b) for a, b in preferred if b < (shard_bits if a == "shard" else rep_bits)]
    steps += [("shard", b) for b in range(shard_bits) if ("shard", b) not in steps]
    steps += [("rep", b) for b in range(rep_bits) if ("rep", b) not in steps]
    return steps


def halving_sum(x, sizes, scatter_steps=4):
    steps = halving_steps(sizes)
    scatter, whole = steps[:scatter_steps], steps[scatter_steps:]
    parts = 1 << len(scatter)
    rows = x.shape[0]
    padded = -(-rows // (parts * 8)) * (parts * 8)
    block = jnp.pad(x, ((0, padded - rows), (0, 0)))
    for axis, bit in scatter:
        upper = ((lax.axis_index(axis) >> bit) & 1) == 1
        half = block.shape[0] // 2
        low, high = block[:half], block[half:]
        keep = jnp.where(upper, high, low)
        give = jnp.where(upper, low, high)
        block = keep + exchange(give, axis, sizes[axis], bit)
    for axis, bit in whole:
        block = block + exchange(block, axis, sizes[axis], bit)
    for axis, bit in reversed(scatter):
        upper = ((lax.axis_index(axis) >> bit) & 1) == 1
        other = exchange(block, axis, sizes[axis], bit)
        block = jnp.where(
            upper, jnp.concatenate([other, block]), jnp.concatenate([block, other])
        )
    return block[:rows]


def shards(
    grad_joined,
    error_joined,
    moment_joined,
    weight_joined,
    factor_joined,
    grad_dense,
    error_dense,
    moment_dense,
    weight_dense,
    factor_dense,
    grad_expand,
    error_expand,
    moment_expand,
    weight_expand,
    factor_expand,
    grad_shrink,
    error_shrink,
    moment_shrink,
    weight_shrink,
    factor_shrink,
    vector_grad,
    vector_moment,
    vector_weight,
):
    replicas = lax.axis_size("rep")
    sizes = {"shard": lax.axis_size("shard"), "rep": replicas}
    first_replica = lax.axis_index("rep") == 0
    gradients = [grad_joined, grad_dense, grad_expand, grad_shrink]
    carried = [error_joined, error_dense, error_expand, error_shrink]
    moment_list = [moment_joined, moment_dense, moment_expand, moment_shrink]
    weight_list = [weight_joined, weight_dense, weight_expand, weight_shrink]
    factors = [factor_joined, factor_dense, factor_expand, factor_shrink]
    members = range(4)
    corrected = [gradients[m][0].astype(jnp.float32) + carried[m][0] for m in members]
    vector_local = vector_grad[0].astype(jnp.float32)
    vector_total = None
    basis_list = []
    for sweep in range(ROUNDS):
        projected = [row_product(factors[m], corrected[m]) for m in members]
        if sweep == 0:
            summed = doubling_sum((*projected, vector_local), "rep")
            vector_total = summed[4]
        else:
            summed = doubling_sum(tuple(projected), "rep")
        grams = [
            jnp.where(first_replica, gram_of(summed[m]), jnp.zeros((), jnp.float32))
            for m in members
        ]
        partials = [mat(summed[m], corrected[m]) for m in members]
        local = jnp.concatenate([p.reshape(-1) for p in partials + grams])
        packed = halving_sum(local.reshape(-1, 128), sizes).reshape(-1)
        shapes = [p.shape for p in partials + grams]
        offsets = [0]
        for shape in shapes:
            offsets.append(offsets[-1] + shape[0] * shape[1])
        pieces = [packed[o : o + a * b].reshape(a, b) for o, (a, b) in zip(offsets, shapes)]
        inverse = inverse_cholesky(jnp.stack(pieces[4:]))
        factors = [mat(inverse[m], pieces[m]) / replicas for m in members]
        basis_list = [mat(inverse[m], summed[m]) for m in members]
    results = []
    for m in members:
        approx = lax.dot_general(
            basis_list[m],
            factors[m],
            (((0,), (0,)), ((), ())),
            precision=HIGHEST_PRECISION,
            preferred_element_type=jnp.float32,
        )
        errors = (corrected[m] - approx)[None]
        moments = momentum_decay * moment_list[m] + approx
        weights = weight_list[m] - learn_rate * moments
        results.extend([errors, moments, weights, factors[m]])
    vector_moments = momentum_decay * vector_moment + vector_total / replicas
    vector_weights = vector_weight - learn_rate * vector_moments
    results.extend([vector_moments, vector_weights])
    return tuple(results)


def solution(mesh):
    big = P("rep", "shard", None)
    rows = P("shard", None)
    member_in = (big, big, rows, rows, P())
    member_out = (big, rows, rows, P())
    return jax.shard_map(
        shards,
        mesh=mesh,
        in_specs=member_in * 4 + (P("rep", "shard"), P("shard"), P("shard")),
        out_specs=member_out * 4 + (P("shard"), P("shard")),
        check_vma=False,
    )
```

profile of v0, /device:TPU:2, one launch (start us, length us, event | category | flops | bytes accessed | tf_op | source)
XLA Modules:
  0.0 286.7 jit_solution(9526776990423639803)
XLA Ops:
  15.5 7.0 %collective-permute-start.2 = (f32[64,128]{1,0:T(8,128)S(1)}, f32[64,128]{1,0:T(8,128)S(1)}, u32[]{:S(2)}, u32[]{:S(2)}) collective-permute-start(f32[64,128]{1,0:T(8,128)S(1)} %fusion.102), channel_id=1, source_target_pairs={{0,128},{32,160},{64,192},{96,224},{128,0},{160,32},{192,64},{224,... | collective-permute-start | bytes 98312 | tf_op jit(solution)/shard_map/ppermute | solution.py:45
  40.6 7.8 %collective-permute-done.4 = f32[608,128]{1,0:T(8,128)S(1)} collective-permute-done((f32[608,128]{1,0:T(8,128)S(1)}, f32[608,128]{1,0:T(8,128)S(1)}, u32[]{:S(2)}, u32[]{:S(2)}) %collective-permute-start.4) | collective-permute-done | bytes 311328 | tf_op jit(solution)/shard_map/ppermute | solution.py:45
  51.2 3.7 %collective-permute-done.5 = f32[304,128]{1,0:T(8,128)S(1)} collective-permute-done((f32[304,128]{1,0:T(8,128)S(1)}, f32[304,128]{1,0:T(8,128)S(1)}, u32[]{:S(2)}, u32[]{:S(2)}) %collective-permute-start.5) | collective-permute-done | bytes 155680 | tf_op jit(solution)/shard_map/ppermute | solution.py:45
  61.6 3.8 %collective-permute-done.7 = f32[152,128]{1,0:T(8,128)S(1)} collective-permute-done((f32[152,128]{1,0:T(8,128)S(1)}, f32[152,128]{1,0:T(8,128)S(1)}, u32[]{:S(2)}, u32[]{:S(2)}) %collective-permute-start.7) | collective-permute-done | bytes 77856 | tf_op jit(solution)/shard_map/ppermute | solution.py:45
  73.4 4.2 %collective-permute-done.9 = f32[152,128]{1,0:T(8,128)S(1)} collective-permute-done((f32[152,128]{1,0:T(8,128)S(1)}, f32[152,128]{1,0:T(8,128)S(1)}, u32[]{:S(2)}, u32[]{:S(2)}) %collective-permute-start.9) | collective-permute-done | bytes 77856 | tf_op jit(solution)/shard_map/ppermute | solution.py:45
  77.6 6.8 %collective-permute-start.10 = (f32[152,128]{1,0:T(8,128)S(1)}, f32[152,128]{1,0:T(8,128)S(1)}, u32[]{:S(2)}, u32[]{:S(2)}) collective-permute-start(f32[152,128]{1,0:T(8,128)S(1)} %add.142), channel_id=1, source_target_pairs={{0,128},{32,160},{64,192},{96,224},{128,0},{160,32},{192,64},{224,... | collective-permute-start | bytes 233480 | tf_op jit(solution)/shard_map/ppermute | solution.py:45
  87.4 4.4 %collective-permute-done.11 = f32[152,128]{1,0:T(8,128)S(1)} collective-permute-done((f32[152,128]{1,0:T(8,128)S(1)}, f32[152,128]{1,0:T(8,128)S(1)}, u32[]{:S(2)}, u32[]{:S(2)}) %collective-permute-start.11) | collective-permute-done | bytes 77856 | tf_op jit(solution)/shard_map/ppermute | solution.py:45
  93.5 3.7 %collective-permute-done.12 = f32[304,128]{1,0:T(8,128)S(1)} collective-permute-done((f32[304,128]{1,0:T(8,128)S(1)}, f32[304,128]{1,0:T(8,128)S(1)}, u32[]{:S(2)}, u32[]{:S(2)}) %collective-permute-start.12) | collective-permute-done | bytes 155680 | tf_op jit(solution)/shard_map/ppermute | solution.py:45
  98.0 6.3 %collective-permute-done.13 = f32[608,128]{1,0:T(8,128)S(1)} collective-permute-done((f32[608,128]{1,0:T(8,128)S(1)}, f32[608,128]{1,0:T(8,128)S(1)}, u32[]{:S(2)}, u32[]{:S(2)}) %collective-permute-start.13) | collective-permute-done | bytes 311328 | tf_op jit(solution)/shard_map/ppermute | solution.py:45
  108.5 11.7 %custom-call.8 = f32[4,32,32]{2,1,0:T(8,128)S(1)} custom-call(f32[4,32,32]{2,1,0:T(8,128)S(1)} %fusion.33), custom_call_target="Cholesky" | custom-call | tf_op jit(solution)/shard_map/jit(cholesky)/cholesky | solution.py:39
  120.4 10.5 %custom-call.9 = f32[4,1,32,32]{2,3,1,0:T(8,128)} custom-call(f32[4,1,32,32]{3,2,1,0:T(8,128)S(1)} %select_bitcast_fusion.1), custom_call_target="InvertDiagBlocksLowerTriangular" | custom-call | tf_op jit(solution)/shard_map/triangular_solve/custom-call.0 | solution.py:41
  141.4 3.9 %collective-permute-done.15 = f32[56,128]{1,0:T(8,128)S(1)} collective-permute-done((f32[56,128]{1,0:T(8,128)S(1)}, f32[56,128]{1,0:T(8,128)S(1)}, u32[]{:S(2)}, u32[]{:S(2)}) %collective-permute-start.15) | collective-permute-done | bytes 28704 | tf_op jit(solution)/shard_map/ppermute | solution.py:45
  146.2 3.8 %collective-permute-done.16 = f32[56,128]{1,0:T(8,128)S(1)} collective-permute-done((f32[56,128]{1,0:T(8,128)S(1)}, f32[56,128]{1,0:T(8,128)S(1)}, u32[]{:S(2)}, u32[]{:S(2)}) %collective-permute-start.16) | collective-permute-done | bytes 28704 | tf_op jit(solution)/shard_map/ppermute | solution.py:45
  150.0 5.6 %collective-permute-start.17 = (f32[56,128]{1,0:T(8,128)S(1)}, f32[56,128]{1,0:T(8,128)S(1)}, u32[]{:S(2)}, u32[]{:S(2)}) collective-permute-start(f32[56,128]{1,0:T(8,128)S(1)} %fusion.101), channel_id=1, source_target_pairs={{0,128},{32,160},{64,192},{96,224},{128,0},{160,32},{192,64},{224,... | collective-permute-start | bytes 86024 | tf_op jit(solution)/shard_map/ppermute | solution.py:45
  172.1 8.9 %collective-permute-done.19 = f32[608,128]{1,0:T(8,128)S(1)} collective-permute-done((f32[608,128]{1,0:T(8,128)S(1)}, f32[608,128]{1,0:T(8,128)S(1)}, u32[]{:S(2)}, u32[]{:S(2)}) %collective-permute-start.19) | collective-permute-done | bytes 311328 | tf_op jit(solution)/shard_map/ppermute | solution.py:45
  182.7 3.7 %collective-permute-done.20 = f32[304,128]{1,0:T(8,128)S(1)} collective-permute-done((f32[304,128]{1,0:T(8,128)S(1)}, f32[304,128]{1,0:T(8,128)S(1)}, u32[]{:S(2)}, u32[]{:S(2)}) %collective-permute-start.20) | collective-permute-done | bytes 155680 | tf_op jit(solution)/shard_map/ppermute | solution.py:45
  186.5 4.4 %collective-permute-done.21 = f32[152,128]{1,0:T(8,128)S(1)} collective-permute-done((f32[152,128]{1,0:T(8,128)S(1)}, f32[152,128]{1,0:T(8,128)S(1)}, u32[]{:S(2)}, u32[]{:S(2)}) %collective-permute-start.21) | collective-permute-done | bytes 77856 | tf_op jit(solution)/shard_map/ppermute | solution.py:45
  193.1 3.8 %collective-permute-done.22 = f32[152,128]{1,0:T(8,128)S(1)} collective-permute-done((f32[152,128]{1,0:T(8,128)S(1)}, f32[152,128]{1,0:T(8,128)S(1)}, u32[]{:S(2)}, u32[]{:S(2)}) %collective-permute-start.22) | collective-permute-done | bytes 77856 | tf_op jit(solution)/shard_map/ppermute | solution.py:45
  204.0 4.9 %collective-permute-done.24 = f32[152,128]{1,0:T(8,128)S(1)} collective-permute-done((f32[152,128]{1,0:T(8,128)S(1)}, f32[152,128]{1,0:T(8,128)S(1)}, u32[]{:S(2)}, u32[]{:S(2)}) %collective-permute-start.24) | collective-permute-done | bytes 77856 | tf_op jit(solution)/shard_map/ppermute | solution.py:45
  209.0 6.3 %collective-permute-start.25 = (f32[152,128]{1,0:T(8,128)S(1)}, f32[152,128]{1,0:T(8,128)S(1)}, u32[]{:S(2)}, u32[]{:S(2)}) collective-permute-start(f32[152,128]{1,0:T(8,128)S(1)} %add.153), channel_id=1, source_target_pairs={{0,128},{32,160},{64,192},{96,224},{128,0},{160,32},{192,64},{224,... | collective-permute-start | bytes 233480 | tf_op jit(solution)/shard_map/ppermute | solution.py:45
  218.3 4.4 %collective-permute-done.26 = f32[152,128]{1,0:T(8,128)S(1)} collective-permute-done((f32[152,128]{1,0:T(8,128)S(1)}, f32[152,128]{1,0:T(8,128)S(1)}, u32[]{:S(2)}, u32[]{:S(2)}) %collective-permute-start.26) | collective-permute-done | bytes 77856 | tf_op jit(solution)/shard_map/ppermute | solution.py:45
  228.7 6.4 %collective-permute-done.28 = f32[608,128]{1,0:T(8,128)S(1)} collective-permute-done((f32[608,128]{1,0:T(8,128)S(1)}, f32[608,128]{1,0:T(8,128)S(1)}, u32[]{:S(2)}, u32[]{:S(2)}) %collective-permute-start.28) | collective-permute-done | bytes 311328 | tf_op jit(solution)/shard_map/ppermute | solution.py:45
  239.2 11.7 %custom-call.10 = f32[4,32,32]{2,1,0:T(8,128)S(1)} custom-call(f32[4,32,32]{2,1,0:T(8,128)S(1)} %fusion.30), custom_call_target="Cholesky" | custom-call | tf_op jit(solution)/shard_map/jit(cholesky)/cholesky | solution.py:39
  252.5 9.8 %custom-call.11 = f32[4,1,32,32]{2,3,1,0:T(8,128)S(1)} custom-call(f32[4,1,32,32]{3,2,1,0:T(8,128)S(1)} %select_bitcast_fusion), custom_call_target="InvertDiagBlocksLowerTriangular" | custom-call | tf_op jit(solution)/shard_map/triangular_solve/custom-call.0 | solution.py:41
  (324 shorter events, 137.5 us)
Async XLA Ops:
  10.3 5.2 %collective-permute-start.1 = (f32[64,128]{1,0:T(8,128)S(1)}, f32[64,128]{1,0:T(8,128)S(1)}, u32[]{:S(2)}, u32[]{:S(2)}) collective-permute-start(f32[64,128]{1,0:T(8,128)S(1)} %fusion.47), channel_id=1, source_target_pairs={{0,64},{32,96},{64,0},{96,32},{128,192},{160,224},{192,128},{224,1... | collective-permute-start | bytes 98312 | tf_op jit(solution)/shard_map/ppermute | solution.py:45
  15.5 8.9 %collective-permute-start.2 = (f32[64,128]{1,0:T(8,128)S(1)}, f32[64,128]{1,0:T(8,128)S(1)}, u32[]{:S(2)}, u32[]{:S(2)}) collective-permute-start(f32[64,128]{1,0:T(8,128)S(1)} %fusion.102), channel_id=1, source_target_pairs={{0,128},{32,160},{64,192},{96,224},{128,0},{160,32},{192,64},{224,... | collective-permute-start | bytes 98312 | tf_op jit(solution)/shard_map/ppermute | solution.py:45
  38.9 9.5 %collective-permute-start.4 = (f32[608,128]{1,0:T(8,128)S(1)}, f32[608,128]{1,0:T(8,128)S(1)}, u32[]{:S(2)}, u32[]{:S(2)}) collective-permute-start(f32[608,128]{1,0:T(8,128)S(1)} %slice_select_fusion.1), channel_id=1, source_target_pairs={{0,2},{1,3},{2,0},{3,1},{4,6},{5,7},{6,4},{7,5},{8,10},{9,11},{10,... | collective-permute-start | bytes 933896 | tf_op jit(solution)/shard_map/ppermute | solution.py:45
  49.5 5.3 %collective-permute-start.5 = (f32[304,128]{1,0:T(8,128)S(1)}, f32[304,128]{1,0:T(8,128)S(1)}, u32[]{:S(2)}, u32[]{:S(2)}) collective-permute-start(f32[304,128]{1,0:T(8,128)S(1)} %slice_select_fusion.3), channel_id=1, source_target_pairs={{0,8},{1,9},{2,10},{3,11},{4,12},{5,13},{6,14},{7,15},{8,0},{9,1},... | collective-permute-start | bytes 466952 | tf_op jit(solution)/shard_map/ppermute | solution.py:45
  54.9 4.5 %collective-permute-start.6 = (f32[152,128]{1,0:T(8,128)S(1)}, f32[152,128]{1,0:T(8,128)S(1)}, u32[]{:S(2)}, u32[]{:S(2)}) collective-permute-start(f32[152,128]{1,0:T(8,128)S(1)} %slice_select_fusion.5), channel_id=1, source_target_pairs={{0,32},{32,0},{64,96},{96,64},{128,160},{160,128},{192,224},{224,1... | collective-permute-start | bytes 233480 | tf_op jit(solution)/shard_map/ppermute | solution.py:45
  59.4 6.0 %collective-permute-start.7 = (f32[152,128]{1,0:T(8,128)S(1)}, f32[152,128]{1,0:T(8,128)S(1)}, u32[]{:S(2)}, u32[]{:S(2)}) collective-permute-start(f32[152,128]{1,0:T(8,128)S(1)} %select_add_fusion.7), channel_id=1, source_target_pairs={{0,4},{1,5},{2,6},{3,7},{4,0},{5,1},{6,2},{7,3},{8,12},{9,13},{10,... | collective-permute-start | bytes 233480 | tf_op jit(solution)/shard_map/ppermute | solution.py:45
  65.4 6.0 %collective-permute-start.8 = (f32[152,128]{1,0:T(8,128)S(1)}, f32[152,128]{1,0:T(8,128)S(1)}, u32[]{:S(2)}, u32[]{:S(2)}) collective-permute-start(f32[152,128]{1,0:T(8,128)S(1)} %add.140), channel_id=1, source_target_pairs={{0,16},{1,17},{2,18},{3,19},{4,20},{5,21},{6,22},{7,23},{8,24},{9,... | collective-permute-start | bytes 233480 | tf_op jit(solution)/shard_map/ppermute | solution.py:45
  71.4 6.2 %collective-permute-start.9 = (f32[152,128]{1,0:T(8,128)S(1)}, f32[152,128]{1,0:T(8,128)S(1)}, u32[]{:S(2)}, u32[]{:S(2)}) collective-permute-start(f32[152,128]{1,0:T(8,128)S(1)} %add.141), channel_id=1, source_target_pairs={{0,64},{32,96},{64,0},{96,32},{128,192},{160,224},{192,128},{224,1... | collective-permute-start | bytes 233480 | tf_op jit(solution)/shard_map/ppermute | solution.py:45
  77.6 9.6 %collective-permute-start.10 = (f32[152,128]{1,0:T(8,128)S(1)}, f32[152,128]{1,0:T(8,128)S(1)}, u32[]{:S(2)}, u32[]{:S(2)}) collective-permute-start(f32[152,128]{1,0:T(8,128)S(1)} %add.142), channel_id=1, source_target_pairs={{0,128},{32,160},{64,192},{96,224},{128,0},{160,32},{192,64},{224,... | collective-permute-start | bytes 233480 | tf_op jit(solution)/shard_map/ppermute | solution.py:45
  87.3 4.5 %collective-permute-start.11 = (f32[152,128]{1,0:T(8,128)S(1)}, f32[152,128]{1,0:T(8,128)S(1)}, u32[]{:S(2)}, u32[]{:S(2)}) collective-permute-start(f32[152,128]{1,0:T(8,128)S(1)} %add.143), channel_id=1, source_target_pairs={{0,32},{32,0},{64,96},{96,64},{128,160},{160,128},{192,224},{224,1... | collective-permute-start | bytes 233480 | tf_op jit(solution)/shard_map/ppermute | solution.py:45
  91.8 5.3 %collective-permute-start.12 = (f32[304,128]{1,0:T(8,128)S(1)}, f32[304,128]{1,0:T(8,128)S(1)}, u32[]{:S(2)}, u32[]{:S(2)}) collective-permute-start(f32[304,128]{1,0:T(8,128)S(1)} %maximum_select_fusion.6), channel_id=1, source_target_pairs={{0,8},{1,9},{2,10},{3,11},{4,12},{5,13},{6,14},{7,15},{8,0},{9,1},... | collective-permute-start | bytes 466952 | tf_op jit(solution)/shard_map/ppermute | solution.py:45
  97.1 7.2 %collective-permute-start.13 = (f32[608,128]{1,0:T(8,128)S(1)}, f32[608,128]{1,0:T(8,128)S(1)}, u32[]{:S(2)}, u32[]{:S(2)}) collective-permute-start(f32[608,128]{1,0:T(8,128)S(1)} %maximum_select_fusion.4), channel_id=1, source_target_pairs={{0,2},{1,3},{2,0},{3,1},{4,6},{5,7},{6,4},{7,5},{8,10},{9,11},{10,... | collective-permute-start | bytes 933896 | tf_op jit(solution)/shard_map/ppermute | solution.py:45
  145.3 4.8 %collective-permute-start.16 = (f32[56,128]{1,0:T(8,128)S(1)}, f32[56,128]{1,0:T(8,128)S(1)}, u32[]{:S(2)}, u32[]{:S(2)}) collective-permute-start(f32[56,128]{1,0:T(8,128)S(1)} %fusion.48), channel_id=1, source_target_pairs={{0,64},{32,96},{64,0},{96,32},{128,192},{160,224},{192,128},{224,1... | collective-permute-start | bytes 86024 | tf_op jit(solution)/shard_map/ppermute | solution.py:45
  150.0 8.0 %collective-permute-start.17 = (f32[56,128]{1,0:T(8,128)S(1)}, f32[56,128]{1,0:T(8,128)S(1)}, u32[]{:S(2)}, u32[]{:S(2)}) collective-permute-start(f32[56,128]{1,0:T(8,128)S(1)} %fusion.101), channel_id=1, source_target_pairs={{0,128},{32,160},{64,192},{96,224},{128,0},{160,32},{192,64},{224,... | collective-permute-start | bytes 86024 | tf_op jit(solution)/shard_map/ppermute | solution.py:45
  171.5 9.5 %collective-permute-start.19 = (f32[608,128]{1,0:T(8,128)S(1)}, f32[608,128]{1,0:T(8,128)S(1)}, u32[]{:S(2)}, u32[]{:S(2)}) collective-permute-start(f32[608,128]{1,0:T(8,128)S(1)} %slice_select_fusion), channel_id=1, source_target_pairs={{0,2},{1,3},{2,0},{3,1},{4,6},{5,7},{6,4},{7,5},{8,10},{9,11},{10,... | collective-permute-start | bytes 933896 | tf_op jit(solution)/shard_map/ppermute | solution.py:45
  181.0 5.3 %collective-permute-start.20 = (f32[304,128]{1,0:T(8,128)S(1)}, f32[304,128]{1,0:T(8,128)S(1)}, u32[]{:S(2)}, u32[]{:S(2)}) collective-permute-start(f32[304,128]{1,0:T(8,128)S(1)} %slice_select_fusion.2), channel_id=1, source_target_pairs={{0,8},{1,9},{2,10},{3,11},{4,12},{5,13},{6,14},{7,15},{8,0},{9,1},... | collective-permute-start | bytes 466952 | tf_op jit(solution)/shard_map/ppermute | solution.py:45
  186.4 4.5 %collective-permute-start.21 = (f32[152,128]{1,0:T(8,128)S(1)}, f32[152,128]{1,0:T(8,128)S(1)}, u32[]{:S(2)}, u32[]{:S(2)}) collective-permute-start(f32[152,128]{1,0:T(8,128)S(1)} %slice_select_fusion.4), channel_id=1, source_target_pairs={{0,32},{32,0},{64,96},{96,64},{128,160},{160,128},{192,224},{224,1... | collective-permute-start | bytes 233480 | tf_op jit(solution)/shard_map/ppermute | solution.py:45
  190.9 6.0 %collective-permute-start.22 = (f32[152,128]{1,0:T(8,128)S(1)}, f32[152,128]{1,0:T(8,128)S(1)}, u32[]{:S(2)}, u32[]{:S(2)}) collective-permute-start(f32[152,128]{1,0:T(8,128)S(1)} %select_add_fusion.6), channel_id=1, source_target_pairs={{0,4},{1,5},{2,6},{3,7},{4,0},{5,1},{6,2},{7,3},{8,12},{9,13},{10,... | collective-permute-start | bytes 233480 | tf_op jit(solution)/shard_map/ppermute | solution.py:45
  196.9 6.2 %collective-permute-start.23 = (f32[152,128]{1,0:T(8,128)S(1)}, f32[152,128]{1,0:T(8,128)S(1)}, u32[]{:S(2)}, u32[]{:S(2)}) collective-permute-start(f32[152,128]{1,0:T(8,128)S(1)} %add.151), channel_id=1, source_target_pairs={{0,16},{1,17},{2,18},{3,19},{4,20},{5,21},{6,22},{7,23},{8,24},{9,... | collective-permute-start | bytes 233480 | tf_op jit(solution)/shard_map/ppermute | solution.py:45
  203.2 5.8 %collective-permute-start.24 = (f32[152,128]{1,0:T(8,128)S(1)}, f32[152,128]{1,0:T(8,128)S(1)}, u32[]{:S(2)}, u32[]{:S(2)}) collective-permute-start(f32[152,128]{1,0:T(8,128)S(1)} %add.152), channel_id=1, source_target_pairs={{0,64},{32,96},{64,0},{96,32},{128,192},{160,224},{192,128},{224,1... | collective-permute-start | bytes 233480 | tf_op jit(solution)/shard_map/ppermute | solution.py:45
  209.0 9.2 %collective-permute-start.25 = (f32[152,128]{1,0:T(8,128)S(1)}, f32[152,128]{1,0:T(8,128)S(1)}, u32[]{:S(2)}, u32[]{:S(2)}) collective-permute-start(f32[152,128]{1,0:T(8,128)S(1)} %add.153), channel_id=1, source_target_pairs={{0,128},{32,160},{64,192},{96,224},{128,0},{160,32},{192,64},{224,... | collective-permute-start | bytes 233480 | tf_op jit(solution)/shard_map/ppermute | solution.py:45
  218.2 4.5 %collective-permute-start.26 = (f32[152,128]{1,0:T(8,128)S(1)}, f32[152,128]{1,0:T(8,128)S(1)}, u32[]{:S(2)}, u32[]{:S(2)}) collective-permute-start(f32[152,128]{1,0:T(8,128)S(1)} %add.154), channel_id=1, source_target_pairs={{0,32},{32,0},{64,96},{96,64},{128,160},{160,128},{192,224},{224,1... | collective-permute-start | bytes 233480 | tf_op jit(solution)/shard_map/ppermute | solution.py:45
  222.7 5.3 %collective-permute-start.27 = (f32[304,128]{1,0:T(8,128)S(1)}, f32[304,128]{1,0:T(8,128)S(1)}, u32[]{:S(2)}, u32[]{:S(2)}) collective-permute-start(f32[304,128]{1,0:T(8,128)S(1)} %maximum_select_fusion.7), channel_id=1, source_target_pairs={{0,8},{1,9},{2,10},{3,11},{4,12},{5,13},{6,14},{7,15},{8,0},{9,1},... | collective-permute-start | bytes 466952 | tf_op jit(solution)/shard_map/ppermute | solution.py:45
  228.1 7.0 %collective-permute-start.28 = (f32[608,128]{1,0:T(8,128)S(1)}, f32[608,128]{1,0:T(8,128)S(1)}, u32[]{:S(2)}, u32[]{:S(2)}) collective-permute-start(f32[608,128]{1,0:T(8,128)S(1)} %maximum_select_fusion.5), channel_id=1, source_target_pairs={{0,2},{1,3},{2,0},{3,1},{4,6},{5,7},{6,4},{7,5},{8,10},{9,11},{10,... | collective-permute-start | bytes 933896 | tf_op jit(solution)/shard_map/ppermute | solution.py:45
  (58 other events, 397.0 us)
where the time goes:
time: 289 us; the launch traced here: 287 us
  waiting for transfers between devices  111 us (38%)
  starting transfers between devices  58.2 us (20%)
  other arithmetic  52.3 us (18%)
  matrix products  36.4 us (13%)
  local copies, waits for them, and re-layouts  26.7 us (9%)
    ppermute x30, waiting for transfers between devices, exchange(): return lax.ppermute(x, axis, [(s, s ^ 1 << bit) for s in range(size)])  111 us
    ppermute x30, starting transfers between devices, exchange(): return lax.ppermute(x, axis, [(s, s ^ 1 << bit) for s in range(size)])  58.2 us
    another operation x7, other arithmetic, inverse_cholesky(): lower = jnp.linalg.cholesky(grams)  24.5 us
    another operation x5, other arithmetic, inverse_cholesky(): return lax.linalg.triangular_solve(lower, eye, left_side=True, lower=True)  21.2 us
    dot_general x20, matrix products, mat(): jnp.dot(a, b, precision=HIGHEST_PRECISION, preferred_element_type=jnp.flo...  18.8 us
    unnamed x121, local copies, waits for them, and re-layouts  8.19 us
    reshape x8, local copies, waits for them, and re-layouts, shards(): packed[o:o + a * b].reshape(a, b)  7.59 us
    dot_general x4, matrix products, shards(): lax.dot_general(basis_list[m], factors[m], (((0,), (0,)), ((), ())), prec...  7.55 us
  transfers between devices with their start and end apart: 30, of which 30 were waited for; matrix products, arithmetic and copies ran while one was open for 0% of the time, Pallas kernels for 0%

commit v1 on v0

--- a/solution.py
+++ b/solution.py
@@ -72,7 +72,7 @@
     return steps
 
 
-def halving_sum(x, sizes, scatter_steps=4):
+def halving_sum(x, sizes, scatter_steps=3):
     steps = halving_steps(sizes)
     scatter, whole = steps[:scatter_steps], steps[scatter_steps:]
     parts = 1 << len(scatter)
@@ -97,7 +97,7 @@
     return block[:rows]
 
 
-def shards(
+def step(
     grad_joined,
     error_joined,
     moment_joined,
@@ -136,12 +136,14 @@
     vector_total = None
     basis_list = []
     for sweep in range(ROUNDS):
-        projected = [row_product(factors[m], corrected[m]) for m in members]
         if sweep == 0:
+            projected = [row_product(factors[m], corrected[m]) for m in members]
             summed = doubling_sum((*projected, vector_local), "rep")
             vector_total = summed[4]
         else:
-            summed = doubling_sum(tuple(projected), "rep")
+            raw = [row_product(pieces[m], corrected[m]) for m in members]
+            raw_sum = doubling_sum(tuple(raw), "rep")
+            summed = [mat(inverse[m], raw_sum[m]) / replicas for m in members]
         grams = [
             jnp.where(first_replica, gram_of(summed[m]), jnp.zeros((), jnp.float32))
             for m in members
@@ -182,7 +184,7 @@
     member_in = (big, big, rows, rows, P())
     member_out = (big, rows, rows, P())
     return jax.shard_map(
-        shards,
+        step,
         mesh=mesh,
         in_specs=member_in * 4 + (P("rep", "shard"), P("shard"), P("shard")),
         out_specs=member_out * 4 + (P("shard"), P("shard")),

time: 289 us -> 286 us (0.990)
  waiting for transfers between devices: 111 us -> 102 us
  starting transfers between devices: 58.2 us -> 65.2 us
    ppermute x30 -> x28, waiting for transfers between devices: 111 us -> 102 us  [exchange(): return lax.ppermute(x, axis, [(s, s ^ 1 << bit) for s in range(size)])]
    ppermute x30 -> x28, starting transfers between devices: 58.2 us -> 65.2 us  [exchange(): return lax.ppermute(x, axis, [(s, s ^ 1 << bit) for s in range(size)])]
    dot_general x20, matrix products: 18.8 us -> 15 us  [mat(): jnp.dot(a, b, precision=HIGHEST_PRECISION, preferred_element_type=jnp.flo...]
    unnamed x121 -> x127, local copies, waits for them, and re-layouts: 8.19 us -> 8.15 us
  transfers between devices with their start and end apart: 30 -> 28, of which waited for: 30 -> 27; matrix products, arithmetic and copies ran while one was open for 0% -> 5% of each run, Pallas kernels for 0% -> 0%
where the time goes in v1:
time: 286 us; the launch traced here: 283 us
  waiting for transfers between devices  102 us (36%)
  starting transfers between devices  65.2 us (23%)
  other arithmetic  54 us (19%)
  matrix products  33.7 us (12%)
  local copies, waits for them, and re-layouts  26.6 us (9%)
    ppermute x28, waiting for transfers between devices, exchange(): return lax.ppermute(x, axis, [(s, s ^ 1 << bit) for s in range(size)])  102 us
    ppermute x28, starting transfers between devices, exchange(): return lax.ppermute(x, axis, [(s, s ^ 1 << bit) for s in range(size)])  65.2 us
    another operation x7, other arithmetic, inverse_cholesky(): lower = jnp.linalg.cholesky(grams)  25.7 us
    another operation x5, other arithmetic, inverse_cholesky(): return lax.linalg.triangular_solve(lower, eye, left_side=True, lower=True)  21.1 us
    dot_general x20, matrix products, mat(): jnp.dot(a, b, precision=HIGHEST_PRECISION, preferred_element_type=jnp.flo...  15 us
    dot_general x8, matrix products, row_product(): lax.dot_general(factor, matrix, (((1,), (1,)), ((), ())), precision=HIGHE...  8.17 us
    unnamed x127, local copies, waits for them, and re-layouts  8.15 us
    reshape x8, local copies, waits for them, and re-layouts, step(): packed[o:o + a * b].reshape(a, b)  7.59 us
  transfers between devices with their start and end apart: 28, of which 27 were waited for; matrix products, arithmetic and copies ran while one was open for 5% of the time, Pallas kernels for 0%

profile of v1, /device:TPU:2, one launch (start us, length us, event | category | flops | bytes accessed | tf_op | source)
XLA Modules:
  0.0 283.5 jit_solution(5387212503465131437)
XLA Ops:
  15.5 7.0 %collective-permute-start.2 = (f32[64,128]{1,0:T(8,128)S(1)}, f32[64,128]{1,0:T(8,128)S(1)}, u32[]{:S(2)}, u32[]{:S(2)}) collective-permute-start(f32[64,128]{1,0:T(8,128)S(1)} %fusion.103), channel_id=1, source_target_pairs={{0,128},{32,160},{64,192},{96,224},{128,0},{160,32},{192,64},{224,... | collective-permute-start | bytes 98312 | tf_op jit(solution)/shard_map/ppermute | solution.py:45
  40.5 7.6 %collective-permute-done.4 = f32[592,128]{1,0:T(8,128)S(1)} collective-permute-done((f32[592,128]{1,0:T(8,128)S(1)}, f32[592,128]{1,0:T(8,128)S(1)}, u32[]{:S(2)}, u32[]{:S(2)}) %collective-permute-start.4) | collective-permute-done | bytes 303136 | tf_op jit(solution)/shard_map/ppermute | solution.py:45
  51.0 3.6 %collective-permute-done.5 = f32[296,128]{1,0:T(8,128)S(1)} collective-permute-done((f32[296,128]{1,0:T(8,128)S(1)}, f32[296,128]{1,0:T(8,128)S(1)}, u32[]{:S(2)}, u32[]{:S(2)}) %collective-permute-start.5) | collective-permute-done | bytes 151584 | tf_op jit(solution)/shard_map/ppermute | solution.py:45
  55.6 4.3 %collective-permute-done.6 = f32[296,128]{1,0:T(8,128)S(1)} collective-permute-done((f32[296,128]{1,0:T(8,128)S(1)}, f32[296,128]{1,0:T(8,128)S(1)}, u32[]{:S(2)}, u32[]{:S(2)}) %collective-permute-start.6) | collective-permute-done | bytes 151584 | tf_op jit(solution)/shard_map/ppermute | solution.py:45
  62.1 4.6 %collective-permute-done.7 = f32[296,128]{1,0:T(8,128)S(1)} collective-permute-done((f32[296,128]{1,0:T(8,128)S(1)}, f32[296,128]{1,0:T(8,128)S(1)}, u32[]{:S(2)}, u32[]{:S(2)}) %collective-permute-start.7) | collective-permute-done | bytes 151584 | tf_op jit(solution)/shard_map/ppermute | solution.py:45
  70.0 3.5 %collective-permute-done.8 = f32[296,128]{1,0:T(8,128)S(1)} collective-permute-done((f32[296,128]{1,0:T(8,128)S(1)}, f32[296,128]{1,0:T(8,128)S(1)}, u32[]{:S(2)}, u32[]{:S(2)}) %collective-permute-start.8) | collective-permute-done | bytes 151584 | tf_op jit(solution)/shard_map/ppermute | solution.py:45
  75.5 5.8 %collective-permute-done.9 = f32[296,128]{1,0:T(8,128)S(1)} collective-permute-done((f32[296,128]{1,0:T(8,128)S(1)}, f32[296,128]{1,0:T(8,128)S(1)}, u32[]{:S(2)}, u32[]{:S(2)}) %collective-permute-start.9) | collective-permute-done | bytes 151584 | tf_op jit(solution)/shard_map/ppermute | solution.py:45
  81.3 9.2 %collective-permute-start.10 = (f32[296,128]{1,0:T(8,128)S(1)}, f32[296,128]{1,0:T(8,128)S(1)}, u32[]{:S(2)}, u32[]{:S(2)}) collective-permute-start(f32[296,128]{1,0:T(8,128)S(1)} %add.143), channel_id=1, source_target_pairs={{0,128},{32,160},{64,192},{96,224},{128,0},{160,32},{192,64},{224,... | collective-permute-start | bytes 454664 | tf_op jit(solution)/shard_map/ppermute | solution.py:45
  95.4 3.6 %collective-permute-done.11 = f32[296,128]{1,0:T(8,128)S(1)} collective-permute-done((f32[296,128]{1,0:T(8,128)S(1)}, f32[296,128]{1,0:T(8,128)S(1)}, u32[]{:S(2)}, u32[]{:S(2)}) %collective-permute-start.11) | collective-permute-done | bytes 151584 | tf_op jit(solution)/shard_map/ppermute | solution.py:45
  100.2 5.8 %collective-permute-done.12 = f32[592,128]{1,0:T(8,128)S(1)} collective-permute-done((f32[592,128]{1,0:T(8,128)S(1)}, f32[592,128]{1,0:T(8,128)S(1)}, u32[]{:S(2)}, u32[]{:S(2)}) %collective-permute-start.12) | collective-permute-done | bytes 303136 | tf_op jit(solution)/shard_map/ppermute | solution.py:45
  110.3 12.4 %custom-call.8 = f32[4,32,32]{2,1,0:T(8,128)} custom-call(f32[4,32,32]{2,1,0:T(8,128)S(1)} %fusion.33), custom_call_target="Cholesky" | custom-call | tf_op jit(solution)/shard_map/jit(cholesky)/cholesky | solution.py:39
  130.5 3.7 %collective-permute-done.14 = f32[56,128]{1,0:T(8,128)S(1)} collective-permute-done((f32[56,128]{1,0:T(8,128)S(1)}, f32[56,128]{1,0:T(8,128)S(1)}, u32[]{:S(2)}, u32[]{:S(2)}) %collective-permute-start.14) | collective-permute-done | bytes 28704 | tf_op jit(solution)/shard_map/ppermute | solution.py:45
  135.6 9.8 %custom-call.9 = f32[4,1,32,32]{2,3,1,0:T(8,128)S(1)} custom-call(f32[4,1,32,32]{3,2,1,0:T(8,128)S(1)} %select_bitcast_fusion.1), custom_call_target="InvertDiagBlocksLowerTriangular" | custom-call | tf_op jit(solution)/shard_map/triangular_solve/custom-call.0 | solution.py:41
  145.5 4.8 %collective-permute-start.16 = (f32[56,128]{1,0:T(8,128)S(1)}, f32[56,128]{1,0:T(8,128)S(1)}, u32[]{:S(2)}, u32[]{:S(2)}) collective-permute-start(f32[56,128]{1,0:T(8,128)S(1)} %fusion.102), channel_id=1, source_target_pairs={{0,128},{32,160},{64,192},{96,224},{128,0},{160,32},{192,64},{224,... | collective-permute-start | bytes 86024 | tf_op jit(solution)/shard_map/ppermute | solution.py:45
  168.6 8.7 %collective-permute-done.18 = f32[592,128]{1,0:T(8,128)S(1)} collective-permute-done((f32[592,128]{1,0:T(8,128)S(1)}, f32[592,128]{1,0:T(8,128)S(1)}, u32[]{:S(2)}, u32[]{:S(2)}) %collective-permute-start.18) | collective-permute-done | bytes 303136 | tf_op jit(solution)/shard_map/ppermute | solution.py:45
  179.1 3.6 %collective-permute-done.19 = f32[296,128]{1,0:T(8,128)S(1)} collective-permute-done((f32[296,128]{1,0:T(8,128)S(1)}, f32[296,128]{1,0:T(8,128)S(1)}, u32[]{:S(2)}, u32[]{:S(2)}) %collective-permute-start.19) | collective-permute-done | bytes 151584 | tf_op jit(solution)/shard_map/ppermute | solution.py:45
  190.2 4.6 %collective-permute-done.21 = f32[296,128]{1,0:T(8,128)S(1)} collective-permute-done((f32[296,128]{1,0:T(8,128)S(1)}, f32[296,128]{1,0:T(8,128)S(1)}, u32[]{:S(2)}, u32[]{:S(2)}) %collective-permute-start.21) | collective-permute-done | bytes 151584 | tf_op jit(solution)/shard_map/ppermute | solution.py:45
  198.1 3.5 %collective-permute-done.22 = f32[296,128]{1,0:T(8,128)S(1)} collective-permute-done((f32[296,128]{1,0:T(8,128)S(1)}, f32[296,128]{1,0:T(8,128)S(1)}, u32[]{:S(2)}, u32[]{:S(2)}) %collective-permute-start.22) | collective-permute-done | bytes 151584 | tf_op jit(solution)/shard_map/ppermute | solution.py:45
  203.3 6.2 %collective-permute-done.23 = f32[296,128]{1,0:T(8,128)S(1)} collective-permute-done((f32[296,128]{1,0:T(8,128)S(1)}, f32[296,128]{1,0:T(8,128)S(1)}, u32[]{:S(2)}, u32[]{:S(2)}) %collective-permute-start.23) | collective-permute-done | bytes 151584 | tf_op jit(solution)/shard_map/ppermute | solution.py:45
  209.6 8.1 %collective-permute-start.24 = (f32[296,128]{1,0:T(8,128)S(1)}, f32[296,128]{1,0:T(8,128)S(1)}, u32[]{:S(2)}, u32[]{:S(2)}) collective-permute-start(f32[296,128]{1,0:T(8,128)S(1)} %add.154), channel_id=1, source_target_pairs={{0,128},{32,160},{64,192},{96,224},{128,0},{160,32},{192,64},{224,... | collective-permute-start | bytes 454664 | tf_op jit(solution)/shard_map/ppermute | solution.py:45
  222.8 3.6 %collective-permute-done.25 = f32[296,128]{1,0:T(8,128)S(1)} collective-permute-done((f32[296,128]{1,0:T(8,128)S(1)}, f32[296,128]{1,0:T(8,128)S(1)}, u32[]{:S(2)}, u32[]{:S(2)}) %collective-permute-start.25) | collective-permute-done | bytes 151584 | tf_op jit(solution)/shard_map/ppermute | solution.py:45
  227.2 6.1 %collective-permute-done.26 = f32[592,128]{1,0:T(8,128)S(1)} collective-permute-done((f32[592,128]{1,0:T(8,128)S(1)}, f32[592,128]{1,0:T(8,128)S(1)}, u32[]{:S(2)}, u32[]{:S(2)}) %collective-permute-start.26) | collective-permute-done | bytes 303136 | tf_op jit(solution)/shard_map/ppermute | solution.py:45
  237.4 11.7 %custom-call.10 = f32[4,32,32]{2,1,0:T(8,128)S(1)} custom-call(f32[4,32,32]{2,1,0:T(8,128)S(1)} %fusion.30), custom_call_target="Cholesky" | custom-call | tf_op jit(solution)/shard_map/jit(cholesky)/cholesky | solution.py:39
  250.7 9.8 %custom-call.11 = f32[4,1,32,32]{2,3,1,0:T(8,128)S(1)} custom-call(f32[4,1,32,32]{3,2,1,0:T(8,128)S(1)} %select_bitcast_fusion), custom_call_target="InvertDiagBlocksLowerTriangular" | custom-call | tf_op jit(solution)/shard_map/triangular_solve/custom-call.0 | solution.py:41
  (322 shorter events, 130.1 us)
Async XLA Ops:
  6.3 4.0 %collective-permute-start = (f32[64,128]{1,0:T(8,128)S(1)}, f32[64,128]{1,0:T(8,128)S(1)}, u32[]{:S(2)}, u32[]{:S(2)}) collective-permute-start(f32[64,128]{1,0:T(8,128)S(1)} %pad_bitcast_fusion), channel_id=1, source_target_pairs={{0,32},{32,0},{64,96},{96,64},{128,160},{160,128},{192,224},{224,1... | collective-permute-start | bytes 98312 | tf_op jit(solution)/shard_map/ppermute | solution.py:45
  10.3 5.2 %collective-permute-start.1 = (f32[64,128]{1,0:T(8,128)S(1)}, f32[64,128]{1,0:T(8,128)S(1)}, u32[]{:S(2)}, u32[]{:S(2)}) collective-permute-start(f32[64,128]{1,0:T(8,128)S(1)} %fusion.45), channel_id=1, source_target_pairs={{0,64},{32,96},{64,0},{96,32},{128,192},{160,224},{192,128},{224,1... | collective-permute-start | bytes 98312 | tf_op jit(solution)/shard_map/ppermute | solution.py:45
  15.5 8.9 %collective-permute-start.2 = (f32[64,128]{1,0:T(8,128)S(1)}, f32[64,128]{1,0:T(8,128)S(1)}, u32[]{:S(2)}, u32[]{:S(2)}) collective-permute-start(f32[64,128]{1,0:T(8,128)S(1)} %fusion.103), channel_id=1, source_target_pairs={{0,128},{32,160},{64,192},{96,224},{128,0},{160,32},{192,64},{224,... | collective-permute-start | bytes 98312 | tf_op jit(solution)/shard_map/ppermute | solution.py:45
  38.8 9.3 %collective-permute-start.4 = (f32[592,128]{1,0:T(8,128)S(1)}, f32[592,128]{1,0:T(8,128)S(1)}, u32[]{:S(2)}, u32[]{:S(2)}) collective-permute-start(f32[592,128]{1,0:T(8,128)S(1)} %slice_select_fusion.1), channel_id=1, source_target_pairs={{0,2},{1,3},{2,0},{3,1},{4,6},{5,7},{6,4},{7,5},{8,10},{9,11},{10,... | collective-permute-start | bytes 909320 | tf_op jit(solution)/shard_map/ppermute | solution.py:45
  49.3 5.3 %collective-permute-start.5 = (f32[296,128]{1,0:T(8,128)S(1)}, f32[296,128]{1,0:T(8,128)S(1)}, u32[]{:S(2)}, u32[]{:S(2)}) collective-permute-start(f32[296,128]{1,0:T(8,128)S(1)} %slice_select_fusion.3), channel_id=1, source_target_pairs={{0,8},{1,9},{2,10},{3,11},{4,12},{5,13},{6,14},{7,15},{8,0},{9,1},... | collective-permute-start | bytes 454664 | tf_op jit(solution)/shard_map/ppermute | solution.py:45
  54.6 5.3 %collective-permute-start.6 = (f32[296,128]{1,0:T(8,128)S(1)}, f32[296,128]{1,0:T(8,128)S(1)}, u32[]{:S(2)}, u32[]{:S(2)}) collective-permute-start(f32[296,128]{1,0:T(8,128)S(1)} %select_add_fusion.5), channel_id=1, source_target_pairs={{0,32},{32,0},{64,96},{96,64},{128,160},{160,128},{192,224},{224,1... | collective-permute-start | bytes 454664 | tf_op jit(solution)/shard_map/ppermute | solution.py:45
  59.9 6.8 %collective-permute-start.7 = (f32[296,128]{1,0:T(8,128)S(1)}, f32[296,128]{1,0:T(8,128)S(1)}, u32[]{:S(2)}, u32[]{:S(2)}) collective-permute-start(f32[296,128]{1,0:T(8,128)S(1)} %add.140), channel_id=1, source_target_pairs={{0,4},{1,5},{2,6},{3,7},{4,0},{5,1},{6,2},{7,3},{8,12},{9,13},{10,... | collective-permute-start | bytes 454664 | tf_op jit(solution)/shard_map/ppermute | solution.py:45
  66.7 6.8 %collective-permute-start.8 = (f32[296,128]{1,0:T(8,128)S(1)}, f32[296,128]{1,0:T(8,128)S(1)}, u32[]{:S(2)}, u32[]{:S(2)}) collective-permute-start(f32[296,128]{1,0:T(8,128)S(1)} %add.141), channel_id=1, source_target_pairs={{0,16},{1,17},{2,18},{3,19},{4,20},{5,21},{6,22},{7,23},{8,24},{9,... | collective-permute-start | bytes 454664 | tf_op jit(solution)/shard_map/ppermute | solution.py:45
  73.5 7.8 %collective-permute-start.9 = (f32[296,128]{1,0:T(8,128)S(1)}, f32[296,128]{1,0:T(8,128)S(1)}, u32[]{:S(2)}, u32[]{:S(2)}) collective-permute-start(f32[296,128]{1,0:T(8,128)S(1)} %add.142), channel_id=1, source_target_pairs={{0,64},{32,96},{64,0},{96,32},{128,192},{160,224},{192,128},{224,1... | collective-permute-start | bytes 454664 | tf_op jit(solution)/shard_map/ppermute | solution.py:45
  81.3 12.4 %collective-permute-start.10 = (f32[296,128]{1,0:T(8,128)S(1)}, f32[296,128]{1,0:T(8,128)S(1)}, u32[]{:S(2)}, u32[]{:S(2)}) collective-permute-start(f32[296,128]{1,0:T(8,128)S(1)} %add.143), channel_id=1, source_target_pairs={{0,128},{32,160},{64,192},{96,224},{128,0},{160,32},{192,64},{224,... | collective-permute-start | bytes 454664 | tf_op jit(solution)/shard_map/ppermute | solution.py:45
  93.8 5.3 %collective-permute-start.11 = (f32[296,128]{1,0:T(8,128)S(1)}, f32[296,128]{1,0:T(8,128)S(1)}, u32[]{:S(2)}, u32[]{:S(2)}) collective-permute-start(f32[296,128]{1,0:T(8,128)S(1)} %add.144), channel_id=1, source_target_pairs={{0,8},{1,9},{2,10},{3,11},{4,12},{5,13},{6,14},{7,15},{8,0},{9,1},... | collective-permute-start | bytes 454664 | tf_op jit(solution)/shard_map/ppermute | solution.py:45
  99.1 6.9 %collective-permute-start.12 = (f32[592,128]{1,0:T(8,128)S(1)}, f32[592,128]{1,0:T(8,128)S(1)}, u32[]{:S(2)}, u32[]{:S(2)}) collective-permute-start(f32[592,128]{1,0:T(8,128)S(1)} %maximum_select_fusion.4), channel_id=1, source_target_pairs={{0,2},{1,3},{2,0},{3,1},{4,6},{5,7},{6,4},{7,5},{8,10},{9,11},{10,... | collective-permute-start | bytes 909320 | tf_op jit(solution)/shard_map/ppermute | solution.py:45
  130.2 3.9 %collective-permute-start.14 = (f32[56,128]{1,0:T(8,128)S(1)}, f32[56,128]{1,0:T(8,128)S(1)}, u32[]{:S(2)}, u32[]{:S(2)}) collective-permute-start(f32[56,128]{1,0:T(8,128)S(1)} %maximum_bitcast_fusion), channel_id=1, source_target_pairs={{0,32},{32,0},{64,96},{96,64},{128,160},{160,128},{192,224},{224,1... | collective-permute-start | bytes 86024 | tf_op jit(solution)/shard_map/ppermute | solution.py:45
  134.2 11.3 %collective-permute-start.15 = (f32[56,128]{1,0:T(8,128)S(1)}, f32[56,128]{1,0:T(8,128)S(1)}, u32[]{:S(2)}, u32[]{:S(2)}) collective-permute-start(f32[56,128]{1,0:T(8,128)S(1)} %fusion.46), channel_id=1, source_target_pairs={{0,64},{32,96},{64,0},{96,32},{128,192},{160,224},{192,128},{224,1... | collective-permute-start | bytes 86024 | tf_op jit(solution)/shard_map/ppermute | solution.py:45
  145.5 7.9 %collective-permute-start.16 = (f32[56,128]{1,0:T(8,128)S(1)}, f32[56,128]{1,0:T(8,128)S(1)}, u32[]{:S(2)}, u32[]{:S(2)}) collective-permute-start(f32[56,128]{1,0:T(8,128)S(1)} %fusion.102), channel_id=1, source_target_pairs={{0,128},{32,160},{64,192},{96,224},{128,0},{160,32},{192,64},{224,... | collective-permute-start | bytes 86024 | tf_op jit(solution)/shard_map/ppermute | solution.py:45
  168.0 9.3 %collective-permute-start.18 = (f32[592,128]{1,0:T(8,128)S(1)}, f32[592,128]{1,0:T(8,128)S(1)}, u32[]{:S(2)}, u32[]{:S(2)}) collective-permute-start(f32[592,128]{1,0:T(8,128)S(1)} %slice_select_fusion), channel_id=1, source_target_pairs={{0,2},{1,3},{2,0},{3,1},{4,6},{5,7},{6,4},{7,5},{8,10},{9,11},{10,... | collective-permute-start | bytes 909320 | tf_op jit(solution)/shard_map/ppermute | solution.py:45
  177.4 5.3 %collective-permute-start.19 = (f32[296,128]{1,0:T(8,128)S(1)}, f32[296,128]{1,0:T(8,128)S(1)}, u32[]{:S(2)}, u32[]{:S(2)}) collective-permute-start(f32[296,128]{1,0:T(8,128)S(1)} %slice_select_fusion.2), channel_id=1, source_target_pairs={{0,8},{1,9},{2,10},{3,11},{4,12},{5,13},{6,14},{7,15},{8,0},{9,1},... | collective-permute-start | bytes 454664 | tf_op jit(solution)/shard_map/ppermute | solution.py:45
  182.7 5.3 %collective-permute-start.20 = (f32[296,128]{1,0:T(8,128)S(1)}, f32[296,128]{1,0:T(8,128)S(1)}, u32[]{:S(2)}, u32[]{:S(2)}) collective-permute-start(f32[296,128]{1,0:T(8,128)S(1)} %select_add_fusion.4), channel_id=1, source_target_pairs={{0,32},{32,0},{64,96},{96,64},{128,160},{160,128},{192,224},{224,1... | collective-permute-start | bytes 454664 | tf_op jit(solution)/shard_map/ppermute | solution.py:45
  188.0 6.8 %collective-permute-start.21 = (f32[296,128]{1,0:T(8,128)S(1)}, f32[296,128]{1,0:T(8,128)S(1)}, u32[]{:S(2)}, u32[]{:S(2)}) collective-permute-start(f32[296,128]{1,0:T(8,128)S(1)} %add.151), channel_id=1, source_target_pairs={{0,4},{1,5},{2,6},{3,7},{4,0},{5,1},{6,2},{7,3},{8,12},{9,13},{10,... | collective-permute-start | bytes 454664 | tf_op jit(solution)/shard_map/ppermute | solution.py:45
  194.8 6.8 %collective-permute-start.22 = (f32[296,128]{1,0:T(8,128)S(1)}, f32[296,128]{1,0:T(8,128)S(1)}, u32[]{:S(2)}, u32[]{:S(2)}) collective-permute-start(f32[296,128]{1,0:T(8,128)S(1)} %add.152), channel_id=1, source_target_pairs={{0,16},{1,17},{2,18},{3,19},{4,20},{5,21},{6,22},{7,23},{8,24},{9,... | collective-permute-start | bytes 454664 | tf_op jit(solution)/shard_map/ppermute | solution.py:45
  201.6 7.9 %collective-permute-start.23 = (f32[296,128]{1,0:T(8,128)S(1)}, f32[296,128]{1,0:T(8,128)S(1)}, u32[]{:S(2)}, u32[]{:S(2)}) collective-permute-start(f32[296,128]{1,0:T(8,128)S(1)} %add.153), channel_id=1, source_target_pairs={{0,64},{32,96},{64,0},{96,32},{128,192},{160,224},{192,128},{224,1... | collective-permute-start | bytes 454664 | tf_op jit(solution)/shard_map/ppermute | solution.py:45
  209.6 11.3 %collective-permute-start.24 = (f32[296,128]{1,0:T(8,128)S(1)}, f32[296,128]{1,0:T(8,128)S(1)}, u32[]{:S(2)}, u32[]{:S(2)}) collective-permute-start(f32[296,128]{1,0:T(8,128)S(1)} %add.154), channel_id=1, source_target_pairs={{0,128},{32,160},{64,192},{96,224},{128,0},{160,32},{192,64},{224,... | collective-permute-start | bytes 454664 | tf_op jit(solution)/shard_map/ppermute | solution.py:45
  220.9 5.5 %collective-permute-start.25 = (f32[296,128]{1,0:T(8,128)S(1)}, f32[296,128]{1,0:T(8,128)S(1)}, u32[]{:S(2)}, u32[]{:S(2)}) collective-permute-start(f32[296,128]{1,0:T(8,128)S(1)} %add.155), channel_id=1, source_target_pairs={{0,8},{1,9},{2,10},{3,11},{4,12},{5,13},{6,14},{7,15},{8,0},{9,1},... | collective-permute-start | bytes 454664 | tf_op jit(solution)/shard_map/ppermute | solution.py:45
  226.4 6.9 %collective-permute-start.26 = (f32[592,128]{1,0:T(8,128)S(1)}, f32[592,128]{1,0:T(8,128)S(1)}, u32[]{:S(2)}, u32[]{:S(2)}) collective-permute-start(f32[592,128]{1,0:T(8,128)S(1)} %maximum_select_fusion.5), channel_id=1, source_target_pairs={{0,2},{1,3},{2,0},{3,1},{4,6},{5,7},{6,4},{7,5},{8,10},{9,11},{10,... | collective-permute-start | bytes 909320 | tf_op jit(solution)/shard_map/ppermute | solution.py:45
  (59 other events, 405.0 us)
